TPU v7x, 256 devices: a whole 4x4x8 slice. The times are simulated.
256 devices in a mesh: seq: 8 (over z_lo, x), chan: 32 (over y, z_hi, core).
Axes of the slice: x: 4, y: 4, z: 8 (z_hi: 4, z_lo: 2; z = z_hi * 2 + z_lo), core: 2. Of those that a mesh axis runs over, the one named last changes fastest.
Arguments:
- tokens: bfloat16 [8192, 4096], P('seq', 'chan'), may hold values from -6 to 6
- in_weight: bfloat16 [4096, 3, 4096], P(None, None, 'chan'), may hold values from -0.09375 to 0.09375
- short_taps: float32 [3, 3, 4096], P(None, None, 'chan'), may hold values from -3 to 3
- filter_taps: float32 [8192, 4096], P('seq', 'chan'), may hold values from -1 to 1
- skip_gain: float32 [4096], P('chan'), may hold values from -4 to 4
- out_weight: bfloat16 [4096, 4096], P('chan'), may hold values from -0.1875 to 0.1875
Outputs:
- layer_out: bfloat16 [8192, 4096], P('seq', 'chan')
All inputs are finite; a program needn't handle non-finite values.
Results may differ from a plain program's by a relative error of at most 0.007.
Values may be sent and summed in bfloat16 or wider, within the bound.
No kernel may reach another device: no remote copies, remote signals or barrier semaphores. Data moves between devices by JAX's collectives and lax.ppermute only.
A program may use at most 128 MiB of HBM per device.

v0:
```python
import math

import jax
import jax.numpy as jnp
from jax import lax
from jax.sharding import PartitionSpec as P

COLS = 256


highest = lax.Precision.HIGHEST


def from_behind(shard, axis, by):
    size = lax.axis_size(axis)
    pairs = [(i, i + by) for i in range(size) if 0 <= i + by < size]
    return lax.ppermute(shard, axis, pairs)


def phase_table(row_count, col_count, period):
    row_index = jnp.arange(row_count, dtype=jnp.int32)[:, None]
    col_index = jnp.arange(col_count, dtype=jnp.int32)[None, :]
    angle = (row_index * col_index % period).astype(jnp.float32) * (2.0 * math.pi / period)
    return (jnp.cos(angle), jnp.sin(angle))


def real_transform(signal, cosine, sines, pattern):
    real_part = jnp.einsum(pattern, cosine, signal, precision=highest)
    imag_part = -jnp.einsum(pattern, sines, signal, precision=highest)
    return (real_part, imag_part)


def complex_transform(real_part, imag_part, cosine, sines, direction, pattern):
    cos_real = jnp.einsum(pattern, cosine, real_part, precision=highest)
    cos_imag = jnp.einsum(pattern, cosine, imag_part, precision=highest)
    sin_real = jnp.einsum(pattern, sines, real_part, precision=highest)
    sin_imag = jnp.einsum(pattern, sines, imag_part, precision=highest)
    return (cos_real - direction * sin_imag, cos_imag + direction * sin_real)


def rotate(real_part, imag_part, cosine, sines, direction):
    return (
        real_part * cosine - direction * imag_part * sines,
        imag_part * cosine + direction * real_part * sines,
    )


def spectrum_product(real_part, imag_part):
    prod_real = real_part[0] * real_part[1] - imag_part[0] * imag_part[1]
    prod_imag = real_part[0] * imag_part[1] + imag_part[0] * real_part[1]
    return (prod_real[None], prod_imag[None])


def real_inverse(real_part, imag_part, cosine, sines, pattern, length):
    return (
        jnp.einsum(pattern, cosine, real_part, precision=highest)
        - jnp.einsum(pattern, sines, imag_part, precision=highest)
    ) / length


def channel_convolve(signal, filter_taps):
    stacked = jnp.stack([signal, filter_taps])
    whole_seq = lax.all_to_all(stacked, "seq", split_axis=2, concat_axis=1, tiled=True)
    length = whole_seq.shape[1]
    narrow = whole_seq.shape[2]
    full_rows = 2 * length // COLS
    half_rows = full_rows // 2
    period = 2 * length
    laid_out = whole_seq.reshape(2, half_rows, COLS, narrow)
    first_cos, first_sin = phase_table(full_rows, half_rows, full_rows)
    real_part, imag_part = real_transform(laid_out, first_cos, first_sin, "kn,xnmc->xkmc")
    twist_cos, twist_sin = phase_table(full_rows, COLS, period)
    twist_cos = twist_cos[:, :, None]
    twist_sin = twist_sin[:, :, None]
    real_part, imag_part = rotate(real_part, imag_part, twist_cos, twist_sin, -1.0)
    second_cos, second_sin = phase_table(COLS, COLS, COLS)
    pattern = "kn,xanc->xakc"
    real_part, imag_part = complex_transform(
        real_part, imag_part, second_cos, second_sin, -1.0, pattern
    )
    real_part, imag_part = spectrum_product(real_part, imag_part)
    real_part, imag_part = complex_transform(
        real_part, imag_part, second_cos, second_sin, 1.0, pattern
    )
    real_part, imag_part = rotate(real_part, imag_part, twist_cos, twist_sin, 1.0)
    last_cos, last_sin = phase_table(half_rows, full_rows, full_rows)
    values = real_inverse(real_part, imag_part, last_cos, last_sin, "nk,xkmc->xnmc", period)
    values = values.reshape(length, narrow)
    return lax.all_to_all(values, "seq", split_axis=0, concat_axis=1, tiled=True)


def body(tokens, in_weight, short_taps, filter_taps, skip_gain, out_weight):
    tok_count = tokens.shape[0]
    chan_count = in_weight.shape[2]
    flat_weight = in_weight.reshape(in_weight.shape[0], 3 * chan_count)
    projected = jnp.dot(
        lax.all_gather(tokens, "chan", axis=1, tiled=True),
        flat_weight,
        preferred_element_type=jnp.float32,
    )
    projected = projected.astype(jnp.bfloat16).reshape(tok_count, 3, chan_count)
    previous = from_behind(projected[-2:], "seq", 1)
    extended = jnp.concatenate([previous, projected], axis=0).astype(jnp.float32)
    short_mixed = (
        short_taps[0] * extended[2:]
        + short_taps[1] * extended[1:-1]
        + short_taps[2] * extended[:-2]
    )
    gate_out = short_mixed[:, 0]
    signal = short_mixed[:, 1] * short_mixed[:, 2]
    convolved = channel_convolve(signal, filter_taps)
    hidden = (gate_out * (convolved + skip_gain * signal)).astype(jnp.bfloat16)
    partial_terms = jnp.dot(hidden, out_weight, preferred_element_type=jnp.float32)
    layer_out = lax.psum_scatter(partial_terms, "chan", scatter_dimension=1, tiled=True)
    return layer_out.astype(jnp.bfloat16)


def solution(mesh):
    in_specs = (
        P("seq", "chan"),
        P(None, None, "chan"),
        P(None, None, "chan"),
        P("seq", "chan"),
        P("chan"),
        P("chan", None),
    )
    out_specs = P("seq", "chan")
    return jax.shard_map(body, mesh=mesh, in_specs=in_specs, out_specs=out_specs, check_vma=False)
```

profile of v0, /device:TPU:35, one launch (start us, length us, event | category | flops | bytes accessed | tf_op | source)
XLA Modules:
  0.0 366.3 jit_solution(10557821155383948905)
XLA Ops:
  6.5 0.0 copy-start
  6.5 0.0 all-gather.2.cloned.1.call-start
  6.5 0.7 all-gather.2.cloned.1.call-update
  7.3 4.8 %copy.29 = bf16[4096,3,128]{0,2,1:T(8,128)(2,1)} copy(bf16[4096,3,128]{2,0,1:T(8,128)(2,1)} %param.7) | data formatting | bytes 6291456 | tf_op args[1]
  12.0 83.7 %all-gather.2.cloned.1.call-done = bf16[1024,4096]{1,0:T(8,128)(2,1)} async-done(((bf16[1024,128]{1,0:T(8,128)(2,1)}), bf16[1024,4096]{1,0:T(8,128)(2,1)}) %all-gather.2.cloned.1.call-update) | async-done | bytes 8388624 | tf_op jit(solution)/shard_map/all_gather | solution.py:97
  95.8 8.8 %convolution_convert_fusion = bf16[1024,384]{1,0:T(8,128)(2,1)S(1)} fusion(bf16[1024,4096]{1,0:T(8,128)(2,1)} %all-gather.2.cloned.1.call-done, bf16[4096,384]{0,1:T(8,128)(2,1)} %bitcast.137), kind=kOutput, calls=%fused_computation.21 | convolution fusion | flops 3221618688 | bytes 12320768 | tf_op jit(solution)/shard_map/dot_general | solution.py:96
  104.7 3.0 collective-permute-start
  107.7 0.0 copy-done.3
  107.7 0.0 copy-done.2
  107.7 0.2 copy.32
  107.9 0.3 copy.30
  108.2 0.8 collective-permute-done
  109.0 0.2 copy.31
  109.2 0.4 maximum_convert_fusion
  109.5 1.2 fusion.14
  110.7 0.1 fusion.45
  110.8 0.1 pad_maximum_fusion
  110.9 1.8 copy.33
  112.7 5.4 %all-to-all-start = ((f32[2,1024,128]{1,0,2:T(2,128)}), f32[2,1024,128]{1,0,2:T(2,128)}, u32[]{:S(2)}, u32[]{:S(2)}) async-start(f32[2,1024,128]{1,0,2:T(2,128)} %copy.33), calls=%async_computation | async-start | bytes 2097152 | tf_op jit(solution)/shard_map/all_to_all | solution.py:63
  118.1 0.5 reduce-scatter.2.cloned.1.call-start
  118.6 0.3 fusion.62
  118.9 0.3 broadcast_multiply_fusion
  119.1 13.5 %all-to-all-done = f32[2,1024,128]{1,0,2:T(2,128)} async-done(((f32[2,1024,128]{1,0,2:T(2,128)}), f32[2,1024,128]{1,0,2:T(2,128)}, u32[]{:S(2)}, u32[]{:S(2)}) %all-to-all-start) | async-done | bytes 1048608 | tf_op jit(solution)/shard_map/all_to_all | solution.py:63
  132.6 1.6 copy.34
  134.2 1.6 copy.35
  135.8 2.5 reshape.85
  138.3 3.2 fusion.70
  141.5 0.0 copy-done.1
  141.5 2.4 fusion
  143.9 3.8 %fusion.2 = f32[2,64,16,256]{3,2,1,0:T(8,128)S(1)} fusion(f32[2,64,256,16]{2,1,3,0:T(8,128)S(1)} %get-tuple-element.6), kind=kOutput, calls=%fused_computation.8 | convolution fusion | flops 1611530240 | bytes 4194304 | tf_op jit(solution)/shard_map/kn,xanc->xakc/dot_general | solution.py:35
  147.8 4.0 %fusion.4 = f32[2,64,16,256]{3,2,1,0:T(8,128)S(1)} fusion(f32[2,64,256,16]{2,1,3,0:T(8,128)S(1)} %get-tuple-element.6), kind=kOutput, calls=%fused_computation.10 | convolution fusion | flops 1611530240 | bytes 4194304 | tf_op jit(solution)/shard_map/kn,xanc->xakc/dot_general | solution.py:37
  151.8 3.9 %subtract_bitcast_fusion = f32[2,64,256,16]{2,3,1,0:T(8,128)S(1)} fusion(f32[2,64,16,256]{3,2,1,0:T(8,128)S(1)} %fusion.4, f32[2,64,256,16]{2,1,3,0:T(8,128)S(1)} %get-tuple-element.5), kind=kOutput, calls=%fused_computation.7 | convolution fusion | flops 1612578816 | bytes 6291456 | tf_op jit(solution)/shard_map/kn,xanc->xakc/dot_general | solution.py:34
  155.7 3.9 %add_bitcast_fusion = f32[2,64,256,16]{2,3,1,0:T(8,128)S(1)} fusion(f32[2,64,16,256]{3,2,1,0:T(8,128)S(1)} %fusion.2, f32[2,64,256,16]{2,1,3,0:T(8,128)S(1)} %get-tuple-element.5), kind=kOutput, calls=%fused_computation.6 | convolution fusion | flops 1612578816 | bytes 6291456 | tf_op jit(solution)/shard_map/kn,xanc->xakc/dot_general | solution.py:36
  159.6 0.6 multiply_subtract_fusion
  160.2 2.0 fusion.24
  162.1 2.2 fusion.20
  164.3 2.0 fusion.16
  166.3 2.1 add_bitcast_fusion.1
  168.5 1.3 fusion.27
  169.8 2.1 fusion.19
  171.9 1.2 all_to_all.28
  173.1 0.3 copy.42
  173.5 12.2 %all_to_all.34 = f32[8,1024,16]{1,2,0:T(8,128)S(1)} all-to-all(f32[8,1024,16]{1,2,0:T(8,128)S(1)} %copy.42), channel_id=1, replica_groups=mesh['seq'=8,'chan'=32] {'seq'}, dimensions={0} | all-to-all | bytes 1048576 | tf_op jit(solution)/shard_map/all_to_all | solution.py:89
  185.7 0.1 fusion.30
  185.8 8.1 %fusion.142 = f32[1024,4096]{1,0:T(8,128)} fusion(bf16[1024,128]{0,1:T(8,128)(2,1)S(1)} %fusion.30, bf16[128,4096]{1,0:T(8,128)(2,1)S(1)} %copy-done), kind=kOutput, calls=%fused_computation.161 | convolution fusion | flops 1073741824 | bytes 18087936 | tf_op jit(solution)/shard_map/dot_general | solution.py:113
  194.0 0.0 reduce-scatter.2.cloned.1.call-update
  194.0 163.5 %reduce-scatter.2.cloned.1.call-done = f32[1024,128]{1,0:T(8,128)} async-done(((f32[1024,4096]{1,0:T(8,128)}), f32[1024,128]{1,0:T(8,128)}) %reduce-scatter.2.cloned.1.call-update) | async-done | bytes 524304 | tf_op jit(solution)/shard_map/reduce_scatter | solution.py:114
  357.5 1.8 convert_element_type.67
  (9 shorter events, 0.0 us)
Async XLA Ops:
  6.5 179.3 %copy-start = (bf16[128,4096]{1,0:T(8,128)(2,1)S(1)}, bf16[128,4096]{1,0:T(8,128)(2,1)}, u32[]{:S(2)}) copy-start(bf16[128,4096]{1,0:T(8,128)(2,1)} %param.11) | copy-start | bytes 3145732
  6.5 89.3 %all-gather.2.cloned.1.call-start = ((), (), s32[]{:S(2)}) async-start(), calls=%async_computation.3 | async-start | bytes 8650752 | tf_op jit(solution)/shard_map/all_gather | solution.py:97
  95.8 11.9 %copy-start.3 = (f32[3,3,128]{2,1,0:T(4,128)S(1)}, f32[3,3,128]{2,1,0:T(4,128)}, u32[]{:S(2)}) copy-start(f32[3,3,128]{2,1,0:T(4,128)} %param.8) | copy-start | bytes 13828
  95.8 11.9 %copy-start.2 = (f32[1024,128]{1,0:T(8,128)S(1)}, f32[1024,128]{1,0:T(8,128)}, u32[]{:S(2)}) copy-start(f32[1024,128]{1,0:T(8,128)} %param.9) | copy-start | bytes 1572868
  104.7 4.3 %collective-permute-start = (bf16[2,3,128]{2,1,0:T(4,128)(2,1)S(1)}, bf16[2,3,128]{2,1,0:T(4,128)(2,1)S(1)}, u32[]{:S(2)}, u32[]{:S(2)}) collective-permute-start(bf16[2,3,128]{2,1,0:T(4,128)(2,1)S(1)} %slice.51), channel_id=1, source_target_pairs={{0,32},{32,64},{64,96},{96,128},{128,160},{160,192},{192,224},{1,3... | collective-permute-start | bytes 4616 | tf_op jit(solution)/shard_map/ppermute | solution.py:17
  112.7 19.9 %all-to-all-start = ((f32[2,1024,128]{1,0,2:T(2,128)}), f32[2,1024,128]{1,0,2:T(2,128)}, u32[]{:S(2)}, u32[]{:S(2)}) async-start(f32[2,1024,128]{1,0,2:T(2,128)} %copy.33), calls=%async_computation | async-start | bytes 2097152 | tf_op jit(solution)/shard_map/all_to_all | solution.py:63
  118.1 239.4 %reduce-scatter.2.cloned.1.call-start = ((), (), s32[]{:S(2)}) async-start(), calls=%async_computation.4 | async-start | bytes 17301504 | tf_op jit(solution)/shard_map/reduce_scatter | solution.py:114
  138.3 3.2 copy-start.1
  171.9 13.8 %copy-start.4 = (f32[128]{0:T(128)S(1)}, f32[128]{0:T(128)}, u32[]{:S(2)}) copy-start(f32[128]{0:T(128)} %param.10) | copy-start | bytes 1540
Sparse Core Ops, SparseCore 0:
  9.8 85.9 all-gather.1
  194.1 163.3 reduce-scatter.1
where the time goes:
time: 374 us; the launch traced here: 366 us
  waiting for transfers between devices  262 us (70%)
  matrix products  49.9 us (13%)
  local copies, waits for them, and re-layouts  14.5 us (4%)
  between operations  13.8 us (4%)
  blocking collectives  12.2 us (3%)
  starting transfers between devices  8.91 us (2%)
  other arithmetic  4.7 us (1%)
    reduce_scatter x1, waiting for transfers between devices, body(): lax.psum_scatter(partial_terms, 'chan', scatter_dimension=1, tiled=True)  164 us
    all_gather x1, waiting for transfers between devices, body(): lax.all_gather(tokens, 'chan', axis=1, tiled=True)  83.7 us
    all_to_all x1, waiting for transfers between devices, channel_convolve(): lax.all_to_all(stacked, 'seq', split_axis=2, concat_axis=1, tiled=True)  13.5 us
    all_to_all x1, blocking collectives, channel_convolve(): lax.all_to_all(values, 'seq', split_axis=0, concat_axis=1, tiled=True)  12.2 us
    dot_general x1, matrix products, body(): jnp.dot(lax.all_gather(tokens, 'chan', axis=1, tiled=True), flat_weight,...  8.84 us
    dot_general x1, matrix products, body(): jnp.dot(hidden, out_weight, preferred_element_type=jnp.float32)  8.12 us
  transfers between devices with their start and end apart: 4, of which 4 were waited for; matrix products, arithmetic and copies ran while one was open for 2% of the time, Pallas kernels for 0%

commit v1 on v0

--- a/solution.py
+++ b/solution.py
@@ -45,10 +45,10 @@
     )
 
 
-def spectrum_product(real_part, imag_part):
-    prod_real = real_part[0] * real_part[1] - imag_part[0] * imag_part[1]
-    prod_imag = real_part[0] * imag_part[1] + imag_part[0] * real_part[1]
-    return (prod_real[None], prod_imag[None])
+def spectrum_product(left, right):
+    prod_real = left[0] * right[0] - left[1] * right[1]
+    prod_imag = left[0] * right[1] + left[1] * right[0]
+    return (prod_real, prod_imag)
 
 
 def real_inverse(real_part, imag_part, cosine, sines, pattern, length):
@@ -58,40 +58,50 @@
     ) / length
 
 
-def channel_convolve(signal, filter_taps):
-    stacked = jnp.stack([signal, filter_taps])
-    whole_seq = lax.all_to_all(stacked, "seq", split_axis=2, concat_axis=1, tiled=True)
-    length = whole_seq.shape[1]
-    narrow = whole_seq.shape[2]
+def tables(length):
     full_rows = 2 * length // COLS
     half_rows = full_rows // 2
     period = 2 * length
-    laid_out = whole_seq.reshape(2, half_rows, COLS, narrow)
-    first_cos, first_sin = phase_table(full_rows, half_rows, full_rows)
-    real_part, imag_part = real_transform(laid_out, first_cos, first_sin, "kn,xnmc->xkmc")
+    first = phase_table(full_rows, half_rows, full_rows)
     twist_cos, twist_sin = phase_table(full_rows, COLS, period)
-    twist_cos = twist_cos[:, :, None]
-    twist_sin = twist_sin[:, :, None]
-    real_part, imag_part = rotate(real_part, imag_part, twist_cos, twist_sin, -1.0)
-    second_cos, second_sin = phase_table(COLS, COLS, COLS)
-    pattern = "kn,xanc->xakc"
+    twist = (twist_cos[:, :, None], twist_sin[:, :, None])
+    second = phase_table(COLS, COLS, COLS)
+    last = phase_table(half_rows, full_rows, full_rows)
+    return first, twist, second, last
+
+
+def forward_spectrum(whole_seq, first, twist, second):
+    length, narrow = whole_seq.shape
+    half_rows = 2 * length // COLS // 2
+    laid_out = whole_seq.reshape(half_rows, COLS, narrow)
+    real_part, imag_part = real_transform(laid_out, first[0], first[1], "kn,nmc->kmc")
+    real_part, imag_part = rotate(real_part, imag_part, twist[0], twist[1], -1.0)
+    return complex_transform(
+        real_part, imag_part, second[0], second[1], -1.0, "kn,anc->akc"
+    )
+
+
+def inverse_spectrum(real_part, imag_part, twist, second, last, length, narrow):
     real_part, imag_part = complex_transform(
-        real_part, imag_part, second_cos, second_sin, -1.0, pattern
+        real_part, imag_part, second[0], second[1], 1.0, "kn,anc->akc"
     )
-    real_part, imag_part = spectrum_product(real_part, imag_part)
-    real_part, imag_part = complex_transform(
-        real_part, imag_part, second_cos, second_sin, 1.0, pattern
-    )
-    real_part, imag_part = rotate(real_part, imag_part, twist_cos, twist_sin, 1.0)
-    last_cos, last_sin = phase_table(half_rows, full_rows, full_rows)
-    values = real_inverse(real_part, imag_part, last_cos, last_sin, "nk,xkmc->xnmc", period)
-    values = values.reshape(length, narrow)
-    return lax.all_to_all(values, "seq", split_axis=0, concat_axis=1, tiled=True)
+    real_part, imag_part = rotate(real_part, imag_part, twist[0], twist[1], 1.0)
+    values = real_inverse(real_part, imag_part, last[0], last[1], "nk,kmc->nmc", 2 * length)
+    return values.reshape(length, narrow)
+
+
+def to_whole_seq(shard):
+    return lax.all_to_all(shard, "seq", split_axis=1, concat_axis=0, tiled=True)
 
 
 def body(tokens, in_weight, short_taps, filter_taps, skip_gain, out_weight):
     tok_count = tokens.shape[0]
     chan_count = in_weight.shape[2]
+    out_block = lax.all_to_all(out_weight, "chan", split_axis=1, concat_axis=0, tiled=True)
+    whole_filter = to_whole_seq(filter_taps)
+    length, narrow = whole_filter.shape
+    first, twist, second, last = tables(length)
+    filter_spec = forward_spectrum(whole_filter, first, twist, second)
     flat_weight = in_weight.reshape(in_weight.shape[0], 3 * chan_count)
     projected = jnp.dot(
         lax.all_gather(tokens, "chan", axis=1, tiled=True),
@@ -108,10 +118,13 @@
     )
     gate_out = short_mixed[:, 0]
     signal = short_mixed[:, 1] * short_mixed[:, 2]
-    convolved = channel_convolve(signal, filter_taps)
+    signal_spec = forward_spectrum(to_whole_seq(signal), first, twist, second)
+    real_part, imag_part = spectrum_product(signal_spec, filter_spec)
+    values = inverse_spectrum(real_part, imag_part, twist, second, last, length, narrow)
+    convolved = lax.all_to_all(values, "seq", split_axis=0, concat_axis=1, tiled=True)
     hidden = (gate_out * (convolved + skip_gain * signal)).astype(jnp.bfloat16)
-    partial_terms = jnp.dot(hidden, out_weight, preferred_element_type=jnp.float32)
-    layer_out = lax.psum_scatter(partial_terms, "chan", scatter_dimension=1, tiled=True)
+    full_hidden = lax.all_gather(hidden, "chan", axis=1, tiled=True)
+    layer_out = jnp.dot(full_hidden, out_block, preferred_element_type=jnp.float32)
     return layer_out.astype(jnp.bfloat16)
 
 

time: 374 us -> 285 us (0.76)
  waiting for transfers between devices: 262 us -> 130 us
  blocking collectives: 12.2 us -> 57.1 us
  starting transfers between devices: 8.91 us -> 13.7 us
    reduce_scatter x1 -> x0, waiting for transfers between devices: 164 us -> none  [body(): lax.psum_scatter(partial_terms, 'chan', scatter_dimension=1, tiled=True)]
    all_gather x0 -> x1, waiting for transfers between devices: none -> 47.5 us  [body(): full_hidden = lax.all_gather(hidden, 'chan', axis=1, tiled=True)]
    all_to_all x1 -> x2, blocking collectives: 12.2 us -> 57.1 us  [the longest x1 45.4 us: body(): lax.all_to_all(out_weight, 'chan', split_axis=1, concat_axis=0, tiled=True)]
    all_to_all x1 -> x2, waiting for transfers between devices: 13.5 us -> 3.49 us  [to_whole_seq(): return lax.all_to_all(shard, 'seq', split_axis=1, concat_axis=0, tiled=True)]
    all_gather x1, waiting for transfers between devices: 83.7 us -> 78.1 us  [body(): lax.all_gather(tokens, 'chan', axis=1, tiled=True)]
    all_to_all x1 -> x2, starting transfers between devices: 5.45 us -> 10.5 us  [to_whole_seq(): return lax.all_to_all(shard, 'seq', split_axis=1, concat_axis=0, tiled=True)]
    dot_general x2 -> x3, matrix products: 5.86 us -> 7.59 us  [complex_transform(): sin_real = jnp.einsum(pattern, sines, real_part, precision=highest)]
  transfers between devices with their start and end apart: 4 -> 5, of which waited for: 4 -> 3; matrix products, arithmetic and copies ran while one was open for 2% -> 8% of each run, Pallas kernels for 0% -> 0%
where the time goes in v1:
time: 285 us; the launch traced here: 281 us
  waiting for transfers between devices  130 us (46%)
  blocking collectives  57.1 us (20%)
  matrix products  50.7 us (18%)
  between operations  13.9 us (5%)
  starting transfers between devices  13.7 us (5%)
  local copies, waits for them, and re-layouts  11.5 us (4%)
  other arithmetic  3.8 us (1%)
    all_gather x1, waiting for transfers between devices, body(): lax.all_gather(tokens, 'chan', axis=1, tiled=True)  78.1 us
    all_gather x1, waiting for transfers between devices, body(): full_hidden = lax.all_gather(hidden, 'chan', axis=1, tiled=True)  47.5 us
    all_to_all x1, blocking collectives, body(): lax.all_to_all(out_weight, 'chan', split_axis=1, concat_axis=0, tiled=True)  45.4 us
    all_to_all x1, blocking collectives, body(): lax.all_to_all(values, 'seq', split_axis=0, concat_axis=1, tiled=True)  11.7 us
    all_to_all x2, starting transfers between devices, to_whole_seq(): return lax.all_to_all(shard, 'seq', split_axis=1, concat_axis=0, tiled=True)  10.5 us
    dot_general x3, matrix products, complex_transform(): sin_real = jnp.einsum(pattern, sines, real_part, precision=highest)  7.59 us
    dot_general x3, matrix products, complex_transform(): sin_imag = jnp.einsum(pattern, sines, imag_part, precision=highest)  7.34 us
    dot_general x1, matrix products, body(): jnp.dot(lax.all_gather(tokens, 'chan', axis=1, tiled=True), flat_weight,...  7 us
  transfers between devices with their start and end apart: 5, of which 3 were waited for; matrix products, arithmetic and copies ran while one was open for 8% of the time, Pallas kernels for 0%

profile of v1, /device:TPU:35, one launch (start us, length us, event | category | flops | bytes accessed | tf_op | source)
XLA Modules:
  0.0 280.6 jit_solution(15404693201254928744)
XLA Ops:
  6.5 0.7 all-gather.3.cloned.1.call-update
  7.3 2.1 copy.44
  9.3 5.2 %all-to-all-start.1 = ((f32[1024,8,16]{0,2,1:T(8,128)}), f32[1024,8,16]{0,2,1:T(8,128)}, u32[]{:S(2)}, u32[]{:S(2)}) async-start(f32[1024,8,16]{0,2,1:T(8,128)} %bitcast.13), calls=%async_computation.1 | async-start | bytes 1048576 | tf_op jit(solution)/shard_map/all_to_all | solution.py:94
  14.5 3.2 %copy.38 = bf16[4096,3,128]{0,2,1:T(8,128)(2,1)S(1)} copy(bf16[4096,3,128]{2,0,1:T(8,128)(2,1)} %param.7) | data formatting | bytes 6291456 | tf_op args[1]
  17.7 78.1 %all-gather.3.cloned.1.call-done = bf16[1024,4096]{1,0:T(8,128)(2,1)} async-done(((bf16[1024,128]{1,0:T(8,128)(2,1)}), bf16[1024,4096]{1,0:T(8,128)(2,1)}) %all-gather.3.cloned.1.call-update) | async-done | bytes 8388624 | tf_op jit(solution)/shard_map/all_gather | solution.py:107
  95.8 7.0 %convolution_convert_fusion = bf16[1024,384]{1,0:T(8,128)(2,1)S(1)} fusion(bf16[1024,4096]{1,0:T(8,128)(2,1)} %all-gather.3.cloned.1.call-done, bf16[4096,384]{0,1:T(8,128)(2,1)S(1)} %bitcast.111), kind=kOutput, calls=%fused_computation.5 | convolution fusion | flops 3221618688 | bytes 12320768 | tf_op jit(solution)/shard_map/dot_general | solution.py:106
  102.8 0.9 copy-done.2
  103.7 3.0 %collective-permute-start = (bf16[2,3,128]{2,1,0:T(4,128)(2,1)S(1)}, bf16[2,3,128]{2,1,0:T(4,128)(2,1)S(1)}, u32[]{:S(2)}, u32[]{:S(2)}) collective-permute-start(bf16[2,3,128]{2,1,0:T(4,128)(2,1)S(1)} %slice.35), channel_id=1, source_target_pairs={{0,32},{32,64},{64,96},{96,128},{128,160},{160,192},{192,224},{1,3... | collective-permute-start | bytes 4616 | tf_op jit(solution)/shard_map/ppermute | solution.py:17
  106.7 1.4 copy.39
  108.2 0.2 copy.40
  108.3 0.4 maximum_convert_fusion
  108.7 1.2 fusion
  109.9 0.9 slice_multiply_fusion.3
  110.8 5.3 %all-to-all-start = ((f32[1024,8,16]{0,2,1:T(8,128)}), f32[1024,8,16]{0,2,1:T(8,128)S(1)}, u32[]{:S(2)}, u32[]{:S(2)}) async-start(f32[1024,8,16]{0,2,1:T(8,128)} %bitcast.8), calls=%async_computation | async-start | bytes 1048576 | tf_op jit(solution)/shard_map/all_to_all | solution.py:94
  116.1 0.2 all-gather.5.cloned.1.call-start
  116.3 0.3 fusion.68
  116.5 0.3 broadcast_multiply_fusion
  116.8 1.4 copy.45
  118.2 0.1 reshape.73
  118.3 2.1 convolution_negate_fusion
  120.4 3.5 %all-to-all-done = f32[1024,8,16]{0,2,1:T(8,128)S(1)} async-done(((f32[1024,8,16]{0,2,1:T(8,128)}), f32[1024,8,16]{0,2,1:T(8,128)S(1)}, u32[]{:S(2)}, u32[]{:S(2)}) %all-to-all-start) | async-done | bytes 524320 | tf_op jit(solution)/shard_map/all_to_all | solution.py:94
  123.9 0.3 copy.41
  124.2 0.1 reshape.72
  124.4 1.1 convolution_negate_fusion.1
  125.5 1.1 fusion.81
  126.6 1.6 multiply_add_fusion.1
  128.2 2.5 fusion.20
  130.7 2.5 fusion.16
  133.2 2.7 fusion.4
  135.9 2.5 fusion.26
  138.3 2.5 fusion.22
  140.8 2.5 fusion.5
  143.3 2.5 fusion.2
  145.8 3.1 %multiply_subtract_fusion = (f32[64,16,256]{2,1,0:T(8,128)S(1)}, f32[64,16,256]{2,1,0:T(8,128)S(1)}) fusion(f32[64,16,256]{2,1,0:T(8,128)S(1)} %fusion.2, f32[64,16,256]{2,1,0:T(8,128)S(1)} %fusion.5, f32[64,16,256]{2,1,0:T(8,128)S(1)} %fusion.4, f32[64,16,256]{2,1,0:T(8,128)S(1)} %fusion.22, f32[64,256,16]{1,0,2:T(8,128)S(1)} %get-tuple-element.14), kind=kOutput, calls=%fused_computation.33 | convolution fusion | flops 808321024 | bytes 7340032 | tf_op jit(solution)/shard_map/kn,anc->akc/dot_general | solution.py:36
  148.9 2.0 fusion.7
  150.9 2.0 fusion.11
  152.9 2.0 convolution_add_fusion
  154.9 2.1 add_bitcast_fusion
  157.0 1.3 fusion.14
  158.3 1.4 fusion.6
  159.9 0.3 copy.54
  160.2 11.7 %all_to_all.67 = f32[8,1024,16]{1,2,0:T(8,128)S(1)} all-to-all(f32[8,1024,16]{1,2,0:T(8,128)S(1)} %copy.54), channel_id=1, replica_groups=mesh['seq'=8,'chan'=32] {'seq'}, dimensions={0} | all-to-all | bytes 1048576 | tf_op jit(solution)/shard_map/all_to_all | solution.py:124
  171.9 0.8 fusion.29
  172.8 0.7 copy.55
  173.5 45.4 %all_to_all.68 = bf16[128,32,128]{0,2,1:T(8,128)(2,1)S(1)} all-to-all(bf16[128,32,128]{0,2,1:T(8,128)(2,1)S(1)} %bitcast.110), channel_id=1, replica_groups=mesh['seq'=8,'chan'=32] {'chan'}, dimensions={1} | all-to-all | bytes 2097152 | tf_op jit(solution)/shard_map/all_to_all | solution.py:100
  218.9 0.7 copy.56
  219.6 47.5 %all-gather.5.cloned.1.call-done = bf16[1024,4096]{0,1:T(8,128)(2,1)} async-done(((bf16[1024,128]{0,1:T(8,128)(2,1)}), bf16[1024,4096]{0,1:T(8,128)(2,1)}) %all-gather.5.cloned.1.call-update) | async-done | bytes 8388624 | tf_op jit(solution)/shard_map/all_gather | solution.py:126
  267.1 6.5 %convolution_convert_fusion.1 = bf16[1024,128]{1,0:T(8,128)(2,1)} fusion(bf16[1024,4096]{0,1:T(8,128)(2,1)} %all-gather.5.cloned.1.call-done, bf16[4096,128]{1,0:T(8,128)(2,1)S(1)} %bitcast.114), kind=kOutput, calls=%fused_computation.20 | convolution fusion | flops 1073872896 | bytes 9699328 | tf_op jit(solution)/shard_map/dot_general | solution.py:127
  (17 shorter events, 0.2 us)
Async XLA Ops:
  6.5 89.3 %all-gather.3.cloned.1.call-start = ((), (), s32[]{:S(2)}) async-start(), calls=%async_computation.4 | async-start | bytes 8650752 | tf_op jit(solution)/shard_map/all_gather | solution.py:107
  9.3 101.5 %all-to-all-start.1 = ((f32[1024,8,16]{0,2,1:T(8,128)}), f32[1024,8,16]{0,2,1:T(8,128)}, u32[]{:S(2)}, u32[]{:S(2)}) async-start(f32[1024,8,16]{0,2,1:T(8,128)} %bitcast.13), calls=%async_computation.1 | async-start | bytes 1048576 | tf_op jit(solution)/shard_map/all_to_all | solution.py:94
  95.8 10.9 %copy-start.3 = (f32[3,3,128]{2,1,0:T(4,128)S(1)}, f32[3,3,128]{2,1,0:T(4,128)}, u32[]{:S(2)}) copy-start(f32[3,3,128]{2,1,0:T(4,128)} %param.8) | copy-start | bytes 13828
  102.8 0.9 copy-start.2
  103.7 4.4 %collective-permute-start = (bf16[2,3,128]{2,1,0:T(4,128)(2,1)S(1)}, bf16[2,3,128]{2,1,0:T(4,128)(2,1)S(1)}, u32[]{:S(2)}, u32[]{:S(2)}) collective-permute-start(bf16[2,3,128]{2,1,0:T(4,128)(2,1)S(1)} %slice.35), channel_id=1, source_target_pairs={{0,32},{32,64},{64,96},{96,128},{128,160},{160,192},{192,224},{1,3... | collective-permute-start | bytes 4616 | tf_op jit(solution)/shard_map/ppermute | solution.py:17
  110.8 13.1 %all-to-all-start = ((f32[1024,8,16]{0,2,1:T(8,128)}), f32[1024,8,16]{0,2,1:T(8,128)S(1)}, u32[]{:S(2)}, u32[]{:S(2)}) async-start(f32[1024,8,16]{0,2,1:T(8,128)} %bitcast.8), calls=%async_computation | async-start | bytes 1048576 | tf_op jit(solution)/shard_map/all_to_all | solution.py:94
  116.1 151.0 %all-gather.5.cloned.1.call-start = ((), (), s32[]{:S(2)}) async-start(), calls=%async_computation.5 | async-start | bytes 8650752 | tf_op jit(solution)/shard_map/all_gather | solution.py:126
  124.4 2.2 copy-start
  159.7 12.2 %copy-start.4 = (f32[128]{0:T(128)S(1)}, f32[128]{0:T(128)}, u32[]{:S(2)}) copy-start(f32[128]{0:T(128)} %param.10) | copy-start | bytes 1540
  160.2 12.6 %copy-start.1 = (bf16[128,4096]{1,0:T(8,128)(2,1)S(1)}, bf16[128,4096]{1,0:T(8,128)(2,1)}, u32[]{:S(2)}) copy-start(bf16[128,4096]{1,0:T(8,128)(2,1)} %param.11) | copy-start | bytes 3145732
Sparse Core Ops, SparseCore 0:
  9.8 85.9 all-gather.2
  172.9 94.0 all-gather.4
